TPU v7x, 32 devices: a whole 2x2x4 slice. The times are simulated.
32 devices in a mesh: rep: 2 (over x), span: 2 (over core), tp: 8 (over z, y).
Axes of the slice: x: 2, y: 2, z: 4, core: 2. Of those that a mesh axis runs over, the one named last changes fastest.
Arguments:
- hidden_in: bfloat16 [16, 128, 6144], P(('rep', 'span'), None, 'tp'), parts along dimension 0, may hold values from -6 to 6
- levels: int32 [16], P(('rep', 'span')), parts along dimension 0, may hold values from 0 to 3
- order: int32 [16], P('rep'), parts along dimension 0, may hold values from 0 to 7, each once
- cache_mask: int32 [16, 8], P('rep'), parts along dimension 0, may hold values 0 or 1
- finished: int32 [2], P('rep'), parts along dimension 0, may hold values from 0 to 7
- cache_kv: bfloat16 [16, 128, 2, 1024], P(('rep', 'span'), None, None, 'tp'), parts along dimension 0, may hold values from -300 to 300
- modulation: bfloat16 [4, 6, 6144], replicated, may hold values from 0.5 to 1.5
- w_qkv: bfloat16 [6144, 3, 1024], P(None, None, 'tp'), may hold values from -0.109375 to 0.109375
- w_out: bfloat16 [1024, 6144], P('tp'), may hold values from -0.375 to 0.375
- w_up: bfloat16 [6144, 4096], P(None, ('span', 'tp')), may hold values from -0.078125 to 0.078125
- w_down: bfloat16 [4096, 6144], P(('span', 'tp')), may hold values from -0.09375 to 0.09375
Outputs:
- layer_out: bfloat16 [16, 128, 6144], P(('rep', 'span'), None, 'tp'), parts along dimension 0
There are 2 independent parts, one for each index of `rep`. A program takes and returns all parts, laid end to end along the dimension named above; an argument that names none is the same for every part. Nothing has to cross between parts.
All inputs are finite; a program needn't handle non-finite values.
Results may differ from a plain program's by a relative error of at most 0.025.
The roundings to bfloat16 on the way count: a program that leaves them out, or rounds other values in their place, can miss the bound.
Values may be sent and summed in bfloat16 or wider, within the bound.
No kernel may reach another device: no remote copies, remote signals or barrier semaphores. Data moves between devices by JAX's collectives and lax.ppermute only.
A program may use at most 128 MiB of HBM per device.

v0:
```python
import math
import jax
import jax.numpy as jnp
from jax import lax
from jax.sharding import PartitionSpec as P

HEAD_DIM = 128
EPSILON = 1e-06
NEGATIVE = -1e30


def normalize(values):
    return values * lax.rsqrt(jnp.mean(values * values, axis=-1, keepdims=True) + EPSILON)


def select_row(source, target):
    matches = jnp.arange(source.shape[0], dtype=jnp.int32) == target
    return jnp.sum(jnp.where(matches.reshape((-1,) + (1,) * (source.ndim - 1)), source, 0), axis=0)


def attend(queries, cache_all, fresh_all, cache_seen, fresh_seen):
    row_count, head_count, head_size = queries.shape
    cache_keys = cache_all[:, :, 0].reshape(-1, head_count, head_size)
    cache_vals = cache_all[:, :, 1].reshape(-1, head_count, head_size)
    fresh_keys = fresh_all[:, :, 0].reshape(-1, head_count, head_size)
    fresh_vals = fresh_all[:, :, 1].reshape(-1, head_count, head_size)
    score_scale = 1.0 / math.sqrt(head_size)
    cache_scores = (
        jnp.einsum("qhd,khd->hqk", queries, cache_keys, preferred_element_type=jnp.float32)
        * score_scale
    )
    fresh_scores = (
        jnp.einsum("qhd,khd->hqk", queries, fresh_keys, preferred_element_type=jnp.float32)
        * score_scale
    )
    cache_scores = jnp.where(cache_seen[None, None, :], cache_scores, NEGATIVE)
    fresh_scores = jnp.where(fresh_seen[None, None, :], fresh_scores, NEGATIVE)
    scores = jnp.concatenate([cache_scores, fresh_scores], axis=2)
    row_max = jnp.max(scores, axis=2, keepdims=True)
    exp_terms = jnp.exp(scores - row_max)
    weights = (exp_terms / jnp.sum(exp_terms, axis=2, keepdims=True)).astype(jnp.bfloat16)
    split_at = cache_keys.shape[0]
    attended = jnp.einsum(
        "hqk,khd->qhd", weights[:, :, :split_at], cache_vals, preferred_element_type=jnp.float32
    )
    attended = attended + jnp.einsum(
        "hqk,khd->qhd", weights[:, :, split_at:], fresh_vals, preferred_element_type=jnp.float32
    )
    return attended.astype(jnp.bfloat16).reshape(row_count, head_count * head_size)


def local(
    hidden_in, levels, order, cache_mask, finished, cache_kv, modulation, w_qkv, w_out, w_up, w_down
):
    span_index = lax.axis_index("span")
    tp_rank = lax.axis_index("tp")
    model_width = modulation.shape[2]
    share_width = hidden_in.shape[2]
    local_count = hidden_in.shape[0]
    row_count = hidden_in.shape[1]
    up_full, down_full = (
        lax.all_gather(w_up, "span", axis=1, tiled=True),
        lax.all_gather(w_down, "span", axis=0, tiled=True),
    )
    mod_table = modulation.reshape(modulation.shape[0], -1)
    picker = (jnp.arange(mod_table.shape[0], dtype=jnp.int32)[None, :] == levels[:, None]).astype(
        jnp.bfloat16
    )
    mod_rows = jnp.dot(picker, mod_table, preferred_element_type=jnp.float32).reshape(
        local_count, 6, model_width
    )
    gathered = lax.all_gather(hidden_in, "tp", axis=2, tiled=True).astype(jnp.float32)
    attn_in = (normalize(gathered) * mod_rows[:, 1][:, None] + mod_rows[:, 0][:, None]).astype(
        jnp.bfloat16
    )
    per_device = w_qkv.shape[2]
    projected = jnp.dot(
        attn_in.reshape(local_count * row_count, model_width),
        w_qkv.reshape(model_width, -1),
        preferred_element_type=jnp.float32,
    )
    projected = projected.astype(jnp.bfloat16).reshape(local_count, row_count, 3, per_device)
    queries = projected[:, :, 0].reshape(local_count, row_count, -1, HEAD_DIM)
    fresh_kv = projected[:, :, 1:]
    cache_all, fresh_all = (
        lax.all_gather(cache_kv, "span", axis=0, tiled=True),
        lax.all_gather(fresh_kv, "span", axis=0, tiled=True),
    )
    positions = jnp.arange(cache_mask.shape[0], dtype=jnp.int32)
    my_spans = span_index * local_count + jnp.arange(local_count, dtype=jnp.int32)
    mask_rows = jax.vmap(lambda target: select_row(cache_mask, target))(my_spans)
    my_order = jax.vmap(lambda target: select_row(order, target))(my_spans)
    cache_seen = jnp.repeat(
        (mask_rows == 1) | (positions[None, :] == finished[0]), row_count, axis=1
    )
    fresh_seen = jnp.repeat(order[None, :] <= my_order[:, None], row_count, axis=1)
    attended = jax.vmap(
        lambda q_rows, c_seen, f_seen: attend(q_rows, cache_all, fresh_all, c_seen, f_seen)
    )(queries, cache_seen, fresh_seen)
    partial_value = jnp.dot(
        attended.reshape(local_count * row_count, -1), w_out, preferred_element_type=jnp.float32
    )
    partial_value = partial_value.reshape(local_count, row_count, model_width)
    mod_share = lax.dynamic_slice_in_dim(mod_rows, tp_rank * share_width, share_width, 2)
    attn_part = lax.psum_scatter(
        partial_value.astype(jnp.bfloat16), "tp", scatter_dimension=2, tiled=True
    ).astype(jnp.float32)
    residual = hidden_in.astype(jnp.float32) + mod_share[:, 2][:, None] * attn_part
    squares = lax.psum(jnp.sum(residual * residual, axis=2), "tp")
    scaled = residual * lax.rsqrt(squares / model_width + EPSILON)[:, :, None]
    mlp_part = (scaled * mod_share[:, 4][:, None] + mod_share[:, 3][:, None]).astype(jnp.bfloat16)
    pre_act = jnp.dot(
        lax.all_gather(mlp_part, "tp", axis=2, tiled=True),
        up_full,
        preferred_element_type=jnp.float32,
    )
    hidden_units = jax.nn.gelu(pre_act).astype(jnp.bfloat16)
    down_terms = jnp.dot(hidden_units, down_full, preferred_element_type=jnp.float32)
    mlp_out = lax.psum_scatter(
        down_terms.astype(jnp.bfloat16), "tp", scatter_dimension=2, tiled=True
    ).astype(jnp.float32)
    result = residual + mod_share[:, 5][:, None] * mlp_out
    return result.astype(jnp.bfloat16)


def solution(mesh):
    placed = (
        P(("rep", "span"), None, "tp"),
        P(("rep", "span")),
        P("rep"),
        P("rep", None),
        P("rep"),
        P(("rep", "span"), None, None, "tp"),
        P(),
        P(None, None, "tp"),
        P("tp", None),
        P(None, ("span", "tp")),
        P(("span", "tp"), None),
    )
    return jax.shard_map(
        local, mesh=mesh, in_specs=placed, out_specs=P(("rep", "span"), None, "tp"), check_vma=False
    )
```

profile of v0, /device:TPU:0, one launch (start us, length us, event | category | flops | bytes accessed | tf_op | source)
XLA Modules:
  0.0 528.1 jit_solution(8121966962387378399)
XLA Ops:
  7.4 0.0 copy-start
  7.4 0.0 all-gather.5.cloned.1.call-start
  7.4 0.7 all-gather.5.cloned.1.call-update
  8.1 0.0 reduce-scatter.3.cloned.1.call-start
  8.1 0.0 copy-start.8
  8.2 0.0 copy-start.10
  8.2 0.0 copy-start.7
  8.2 0.0 copy-start.6
  8.2 0.0 copy-start.9
  8.2 6.8 %copy.29 = bf16[6144,3,128]{0,2,1:T(8,128)(2,1)} copy(bf16[6144,3,128]{2,0,1:T(8,128)(2,1)} %param.18) | data formatting | bytes 9437184 | tf_op args[7]
  15.6 0.1 iota_compare_fusion
  15.7 0.0 copy-done.8
  15.7 0.1 select_reduce_fusion
  15.8 0.1 broadcast_bitcast_fusion.1
  15.9 0.0 copy-done.10
  15.9 0.2 select_reduce_fusion.1
  16.1 0.1 broadcast_compare_fusion
  16.2 0.1 broadcast_bitcast_fusion
  16.3 0.0 copy-done.7
  16.3 2.3 all_gather.19
  18.6 0.0 copy-done.6
  18.6 0.4 fusion.30
  19.0 93.2 %all-gather.5.cloned.1.call-done = bf16[4,128,6144]{2,1,0:T(8,128)(2,1)} async-done(((bf16[4,128,768]{2,1,0:T(8,128)(2,1)}), bf16[4,128,6144]{2,1,0:T(8,128)(2,1)}) %all-gather.5.cloned.1.call-update) | async-done | bytes 6291472 | tf_op jit(solution)/shard_map/all_gather | solution.py:72
  112.2 4.2 fusion
  116.4 0.3 copy-done.2
  116.8 2.7 fusion.3
  119.5 5.8 %convolution_convert_fusion.2 = bf16[512,384]{1,0:T(8,128)(2,1)S(1)} fusion(bf16[512,6144]{1,0:T(8,128)(2,1)S(1)} %bitcast.110, bf16[6144,384]{0,1:T(8,128)(2,1)} %bitcast.111), kind=kOutput, calls=%fused_computation.27 | convolution fusion | flops 2416115712 | bytes 11403264 | tf_op jit(solution)/shard_map/dot_general | solution.py:77
  125.3 0.2 copy.30
  125.5 0.1 reshape.192
  125.6 0.1 slice.60
  125.8 0.2 copy.33
  126.0 2.4 all_gather.20
  128.4 0.1 copy.39
  128.5 0.4 fusion.32
  129.0 0.8 fusion.9
  129.8 0.7 fusion.8
  130.5 0.9 divide_convert_fusion
  131.5 1.3 copy-done.5
  132.8 0.4 fusion.29
  133.2 0.0 copy-done
  133.2 5.4 %convolution_convert_fusion.1 = bf16[4,128,6144]{2,1,0:T(8,128)(2,1)} fusion(bf16[128,6144]{1,0:T(8,128)(2,1)S(1)} %copy-done, f32[128,4,128]{0,2,1:T(8,128)S(1)} %fusion.29, bf16[1024,128,1]{1,0,2:T(8,128)(2,1)S(1)} %bitcast.112, bf16[4,1,128,2048]{3,2,0,1:T(8,128)(2,1)} %copy-done.5), kind=kOutput, calls=%fused_computation.7 | convolution fusion | flops 942800896 | bytes 9437184 | tf_op jit(solution)/shard_map/dot_general | solution.py:100
  138.7 0.0 reduce-scatter.3.cloned.1.call-update
  138.7 0.0 copy-start.3
  138.7 0.0 all-gather.9.cloned.1.call-start
  138.7 0.5 all-gather.9.cloned.1.call-update
  139.3 0.0 all-gather.7.cloned.1.call-start
  139.4 115.7 %reduce-scatter.3.cloned.1.call-done = bf16[4,128,768]{2,1,0:T(8,128)(2,1)} async-done(((bf16[4,128,6144]{2,1,0:T(8,128)(2,1)}), bf16[4,128,768]{2,1,0:T(8,128)(2,1)}) %reduce-scatter.3.cloned.1.call-update) | async-done | bytes 786448 | tf_op jit(solution)/shard_map/reduce_scatter | solution.py:105
  255.1 1.5 multiply_reduce_fusion
  256.6 19.6 %psum.7 = f32[4,128]{1,0:T(4,128)S(1)} all-reduce(f32[4,128]{1,0:T(4,128)S(1)} %multiply_reduce_fusion), channel_id=1, replica_groups=mesh['rep'=2,'span'=2,'tp'=8] {'tp'}, use_global_device_ids=true, to_apply=%region_8.9 | all-reduce | flops 512 | bytes 4096 | tf_op jit(solution)/shard_map/psum | solution.py:109
  276.2 2.4 add_convert_fusion.1
  278.6 0.0 all-gather.7.cloned.1.call-update
  278.6 0.0 all-gather.11.cloned.1.call-start
  278.7 0.5 all-gather.11.cloned.1.call-update
  279.2 0.0 reduce-scatter.5.cloned.1.call-start
  279.3 0.0 all-gather.9.cloned.1.call-done
  279.3 95.3 %all-gather.7.cloned.1.call-done = bf16[4,128,6144]{2,1,0:T(8,128)(2,1)} async-done(((bf16[4,128,768]{2,1,0:T(8,128)(2,1)}), bf16[4,128,6144]{2,1,0:T(8,128)(2,1)}) %all-gather.7.cloned.1.call-update) | async-done | bytes 6291472 | tf_op jit(solution)/shard_map/all_gather | solution.py:113
  374.6 8.2 %fusion.26 = bf16[4,128,512]{2,1,0:T(8,128)(2,1)S(1)} fusion(bf16[4,128,6144]{2,1,0:T(8,128)(2,1)} %all-gather.7.cloned.1.call-done, bf16[6144,512]{1,0:T(8,128)(2,1)} %all-gather.9.cloned.1.call-done), kind=kOutput, calls=%fused_computation.39 | convolution fusion | flops 3223584768 | bytes 13107200 | tf_op jit(solution)/shard_map/dot_general | solution.py:112
  382.8 8.3 %all-gather.11.cloned.1.call-done = bf16[512,6144]{1,0:T(8,128)(2,1)} async-done(((bf16[256,6144]{1,0:T(8,128)(2,1)}), bf16[512,6144]{1,0:T(8,128)(2,1)}) %all-gather.11.cloned.1.call-update) | async-done | bytes 6291472 | tf_op jit(solution)/shard_map/all_gather | solution.py:63
  391.1 8.1 %convolution_convert_fusion = bf16[4,128,6144]{2,1,0:T(8,128)(2,1)} fusion(bf16[4,128,512]{2,1,0:T(8,128)(2,1)S(1)} %fusion.26, bf16[512,6144]{1,0:T(8,128)(2,1)} %all-gather.11.cloned.1.call-done), kind=kOutput, calls=%fused_computation.6 | convolution fusion | flops 3224371200 | bytes 13107200 | tf_op jit(solution)/shard_map/dot_general | solution.py:118
  399.1 0.0 reduce-scatter.5.cloned.1.call-update
  399.2 0.0 copy-start.1
  399.2 118.9 %reduce-scatter.5.cloned.1.call-done = bf16[4,128,768]{2,1,0:T(8,128)(2,1)} async-done(((bf16[4,128,6144]{2,1,0:T(8,128)(2,1)}), bf16[4,128,768]{2,1,0:T(8,128)(2,1)}) %reduce-scatter.5.cloned.1.call-update) | async-done | bytes 786448 | tf_op jit(solution)/shard_map/reduce_scatter | solution.py:119
  518.1 0.0 copy-done.4
  518.1 2.4 add_convert_fusion
  (20 shorter events, 0.3 us)
Async XLA Ops:
  7.4 125.9 %copy-start = (bf16[128,6144]{1,0:T(8,128)(2,1)S(1)}, bf16[128,6144]{1,0:T(8,128)(2,1)}, u32[]{:S(2)}) copy-start(bf16[128,6144]{1,0:T(8,128)(2,1)} %param.19) | copy-start | bytes 4718596
  7.4 104.8 %all-gather.5.cloned.1.call-start = ((), (), s32[]{:S(2)}) async-start(), calls=%async_computation.2 | async-start | bytes 7077888 | tf_op jit(solution)/shard_map/all_gather | solution.py:72
  8.1 247.0 %reduce-scatter.3.cloned.1.call-start = ((), (), s32[]{:S(2)}) async-start(), calls=%async_computation.3 | async-start | bytes 7077888 | tf_op jit(solution)/shard_map/reduce_scatter | solution.py:105
  8.1 7.6 %copy-start.8 = (s32[8,8]{1,0:T(8,128)S(1)}, s32[8,8]{1,0:T(8,128)}, u32[]{:S(2)}) copy-start(s32[8,8]{1,0:T(8,128)} %param.14) | copy-start | bytes 772
  8.2 7.7 %copy-start.10 = (s32[8]{0:T(128)S(1)}, s32[8]{0:T(128)}, u32[]{:S(2)}) copy-start(s32[8]{0:T(128)} %param.13) | copy-start | bytes 100
  8.2 8.1 %copy-start.7 = (bf16[4,128,2,128]{3,2,1,0:T(2,128)(2,1)S(1)}, bf16[4,128,2,128]{3,2,1,0:T(2,128)(2,1)}, u32[]{:S(2)}) copy-start(bf16[4,128,2,128]{3,2,1,0:T(2,128)(2,1)} %param.16) | copy-start | bytes 786436
  8.2 10.4 %copy-start.6 = (bf16[4,6,6144]{2,0,1:T(4,128)(2,1)S(1)}, bf16[4,6,6144]{2,0,1:T(4,128)(2,1)}, u32[]{:S(2)}) copy-start(bf16[4,6,6144]{2,0,1:T(4,128)(2,1)} %param.17) | copy-start | bytes 884740
  8.2 10.4 %copy-start.9 = (s32[4]{0:T(128)S(1)}, s32[4]{0:T(128)}, u32[]{:S(2)}) copy-start(s32[4]{0:T(128)} %param.12) | copy-start | bytes 52
  112.2 4.6 copy-start.2
  131.4 1.3 copy-start.5
  138.7 116.4 %copy-start.3 = (bf16[4,128,768]{2,1,0:T(8,128)(2,1)S(1)}, bf16[4,128,768]{2,1,0:T(8,128)(2,1)}, u32[]{:S(2)}) copy-start(bf16[4,128,768]{2,1,0:T(8,128)(2,1)} %param.11) | copy-start | bytes 2359300
  138.7 140.6 %all-gather.9.cloned.1.call-start = ((), (), s32[]{:S(2)}) async-start(), calls=%async_computation.5 | async-start | bytes 9437184 | tf_op jit(solution)/shard_map/all_gather | solution.py:62
  139.3 235.3 %all-gather.7.cloned.1.call-start = ((), (), s32[]{:S(2)}) async-start(), calls=%async_computation.4 | async-start | bytes 7077888 | tf_op jit(solution)/shard_map/all_gather | solution.py:113
  278.6 112.4 %all-gather.11.cloned.1.call-start = ((), (), s32[]{:S(2)}) async-start(), calls=%async_computation.6 | async-start | bytes 9437184 | tf_op jit(solution)/shard_map/all_gather | solution.py:63
  279.2 238.9 %reduce-scatter.5.cloned.1.call-start = ((), (), s32[]{:S(2)}) async-start(), calls=%async_computation.7 | async-start | bytes 7077888 | tf_op jit(solution)/shard_map/reduce_scatter | solution.py:119
  399.1 119.0 %copy-start.4 = (bf16[4,128,768]{2,1,0:T(8,128)(2,1)S(1)}, bf16[4,128,768]{2,1,0:T(8,128)(2,1)}, u32[]{:S(2)}) copy-start(bf16[4,128,768]{2,1,0:T(8,128)(2,1)} %reduce-scatter.3.cloned.1.call-done) | copy-start | bytes 2359300
  399.2 121.3 %copy-start.1 = (bf16[128,6144]{1,0:T(8,128)(2,1)S(1)}, bf16[128,6144]{1,0:T(8,128)(2,1)}, u32[]{:S(2)}) copy-start(bf16[128,6144]{1,0:T(8,128)(2,1)} %param.19) | copy-start | bytes 4718596
Sparse Core Ops, SparseCore 0:
  10.4 101.7 all-gather.4
  138.8 116.2 reduce-scatter.2
Sparse Core Ops, SparseCore 1:
  140.7 13.8 all-gather.8
  278.7 95.8 all-gather.6
  376.0 15.0 all-gather.10
  399.2 118.8 reduce-scatter.4
where the time goes:
time: 529 us; the launch traced here: 528 us
  waiting for transfers between devices  433 us (82%)
  matrix products  29.6 us (6%)
  blocking collectives  24.2 us (5%)
  between operations  16 us (3%)
  other arithmetic  15.4 us (3%)
  local copies, waits for them, and re-layouts  9.57 us (2%)
    reduce_scatter x1, waiting for transfers between devices, local(): lax.psum_scatter(down_terms.astype(jnp.bfloat16), 'tp', scatter_dimension...  119 us
    reduce_scatter x1, waiting for transfers between devices, local(): lax.psum_scatter(partial_value.astype(jnp.bfloat16), 'tp', scatter_dimens...  116 us
    all_gather x1, waiting for transfers between devices, local(): lax.all_gather(mlp_part, 'tp', axis=2, tiled=True)  95.3 us
    all_gather x1, waiting for transfers between devices, local(): lax.all_gather(hidden_in, 'tp', axis=2, tiled=True).astype(jnp.float32)  93.2 us
    psum x1, blocking collectives, local(): squares = lax.psum(jnp.sum(residual * residual, axis=2), 'tp')  19.6 us
  transfers between devices with their start and end apart: 6, of which 5 were waited for; matrix products, arithmetic and copies ran while one was open for 4% of the time, Pallas kernels for 0%

commit v1 on v0

--- a/solution.py
+++ b/solution.py
@@ -7,6 +7,28 @@
 HEAD_DIM = 128
 EPSILON = 1e-06
 NEGATIVE = -1e30
+
+
+def in_order(pieces, dim):
+    shape = list(pieces.shape[1:])
+    shape[dim] *= pieces.shape[0]
+    return jnp.moveaxis(pieces, 0, dim).reshape(shape)
+
+
+def gather_around(x, axis, dim):
+    count = lax.axis_size(axis)
+    pairs = [(i, (i + 1) % count) for i in range(count)]
+    back = [(b, a) for a, b in pairs]
+    lower, upper = ([], [])
+    for step in range(count - 1):
+        if step % 2 == 0:
+            lower.append(lax.ppermute(lower[-1] if lower else x, axis, pairs))
+        else:
+            upper.append(lax.ppermute(upper[-1] if upper else x, axis, back))
+    blocks = jnp.stack([*lower[::-1], x, *upper])
+    shift = lax.axis_index(axis) - len(lower)
+    blocks = blocks[(jnp.arange(count) - shift) % count]
+    return in_order(blocks, dim)
 
 
 def normalize(values):
@@ -69,7 +91,7 @@
     mod_rows = jnp.dot(picker, mod_table, preferred_element_type=jnp.float32).reshape(
         local_count, 6, model_width
     )
-    gathered = lax.all_gather(hidden_in, "tp", axis=2, tiled=True).astype(jnp.float32)
+    gathered = gather_around(hidden_in, "tp", 2).astype(jnp.float32)
     attn_in = (normalize(gathered) * mod_rows[:, 1][:, None] + mod_rows[:, 0][:, None]).astype(
         jnp.bfloat16
     )

time: 529 us -> 605 us (1.14)
  local copies, waits for them, and re-layouts: 9.57 us -> 53.7 us
  starting transfers between devices: 0.21 us -> 15.6 us
  other arithmetic: 15.4 us -> 29.3 us
    all_gather x1 -> x0, waiting for transfers between devices: 93.2 us -> none  [local(): lax.all_gather(hidden_in, 'tp', axis=2, tiled=True).astype(jnp.float32)]
    ppermute x0 -> x7, waiting for transfers between devices: none -> 92.2 us  [the longest x4 67.7 us: gather_around(): lower.append(lax.ppermute(lower[-1] if lower else x, axis, pairs))]
    convert_element_type x0 -> x2, local copies, waits for them, and re-layouts: none -> 21.3 us  [the longest x1 12.6 us: local(): gathered = gather_around(hidden_in, 'tp', 2).astype(jnp.float32)]
    ppermute x0 -> x7, starting transfers between devices: none -> 15.4 us  [the longest x4 7.93 us: gather_around(): lower.append(lax.ppermute(lower[-1] if lower else x, axis, pairs))]
    unnamed x29 -> x44, local copies, waits for them, and re-layouts: 8.82 us -> 19.9 us
    convert_element_type x0 -> x1, other arithmetic: none -> 8.98 us  [local(): gathered = gather_around(hidden_in, 'tp', 2).astype(jnp.float32)]
    convert_element_type x1, other arithmetic: 2.7 us -> 9.85 us  [local(): (normalize(gathered) * mod_rows[:, 1][:, None] + mod_rows[:, 0][:, None])...]
    gather x0 -> x1, local copies, waits for them, and re-layouts: none -> 6.37 us  [gather_around(): blocks = blocks[(jnp.arange(count) - shift) % count]]
  transfers between devices with their start and end apart: 6 -> 12, of which waited for: 5 -> 9; matrix products, arithmetic and copies ran while one was open for 4% -> 6% of each run, Pallas kernels for 0% -> 0%
where the time goes in v1:
time: 605 us; the launch traced here: 604 us
  waiting for transfers between devices  433 us (72%)
  local copies, waits for them, and re-layouts  53.7 us (9%)
  matrix products  32.3 us (5%)
  other arithmetic  29.3 us (5%)
  blocking collectives  24.2 us (4%)
  between operations  15.9 us (3%)
  starting transfers between devices  15.6 us (3%)
    reduce_scatter x1, waiting for transfers between devices, local(): lax.psum_scatter(down_terms.astype(jnp.bfloat16), 'tp', scatter_dimension...  119 us
    reduce_scatter x1, waiting for transfers between devices, local(): lax.psum_scatter(partial_value.astype(jnp.bfloat16), 'tp', scatter_dimens...  116 us
    all_gather x1, waiting for transfers between devices, local(): lax.all_gather(mlp_part, 'tp', axis=2, tiled=True)  95.3 us
    ppermute x4, waiting for transfers between devices, gather_around(): lower.append(lax.ppermute(lower[-1] if lower else x, axis, pairs))  67.7 us
    ppermute x3, waiting for transfers between devices, gather_around(): upper.append(lax.ppermute(upper[-1] if upper else x, axis, back))  24.5 us
    unnamed x44, local copies, waits for them, and re-layouts  19.9 us
    psum x1, blocking collectives, local(): squares = lax.psum(jnp.sum(residual * residual, axis=2), 'tp')  19.6 us
    convert_element_type x1, local copies, waits for them, and re-layouts, local(): gathered = gather_around(hidden_in, 'tp', 2).astype(jnp.float32)  12.6 us
  transfers between devices with their start and end apart: 12, of which 9 were waited for; matrix products, arithmetic and copies ran while one was open for 6% of the time, Pallas kernels for 0%

profile of v1, /device:TPU:0, one launch (start us, length us, event | category | flops | bytes accessed | tf_op | source)
XLA Modules:
  0.0 603.6 jit_solution(10436621663848118650)
XLA Ops:
  7.4 3.0 collective-permute-start
  10.3 3.1 collective-permute-start.4
  14.1 0.1 iota_compare_fusion
  14.2 0.8 select_reduce_fusion
  14.9 1.3 fusion.30
  16.3 28.0 %collective-permute-done = bf16[4,128,768]{2,1,0:T(8,128)(2,1)S(1)} collective-permute-done((bf16[4,128,768]{2,1,0:T(8,128)(2,1)}, bf16[4,128,768]{2,1,0:T(8,128)(2,1)S(1)}, u32[]{:S(2)}, u32[]{:S(2)}) %collective-permute-start) | collective-permute-done | bytes 786464 | tf_op jit(solution)/shard_map/ppermute | solution.py:25
  44.3 2.4 collective-permute-start.1
  46.7 0.7 slice_bitcast_fusion.6
  47.3 19.0 %collective-permute-done.1 = bf16[4,128,768]{2,1,0:T(8,128)(2,1)S(1)} collective-permute-done((bf16[4,128,768]{2,1,0:T(8,128)(2,1)S(1)}, bf16[4,128,768]{2,1,0:T(8,128)(2,1)S(1)}, u32[]{:S(2)}, u32[]{:S(2)}) %collective-permute-start.1) | collective-permute-done | bytes 786464 | tf_op jit(solution)/shard_map/ppermute | solution.py:25
  66.4 7.0 %copy.41 = bf16[6144,3,128]{0,2,1:T(8,128)(2,1)} copy(bf16[6144,3,128]{2,0,1:T(8,128)(2,1)} %param.18) | data formatting | bytes 9437184 | tf_op args[7]
  73.4 0.1 broadcast_bitcast_fusion.1
  73.5 0.2 select_reduce_fusion.1
  73.7 0.1 broadcast_compare_fusion
  73.8 4.4 collective-permute-start.5
  78.2 20.6 %collective-permute-done.2 = bf16[4,128,768]{2,1,0:T(8,128)(2,1)} collective-permute-done((bf16[4,128,768]{2,1,0:T(8,128)(2,1)S(1)}, bf16[4,128,768]{2,1,0:T(8,128)(2,1)}, u32[]{:S(2)}, u32[]{:S(2)}) %collective-permute-start.2) | collective-permute-done | bytes 786464 | tf_op jit(solution)/shard_map/ppermute | solution.py:25
  98.8 2.6 collective-permute-start.3
  101.4 0.1 broadcast_bitcast_fusion
  101.6 2.3 all_gather.15
  103.9 0.7 fusion.41
  104.6 16.0 %collective-permute-done.5 = bf16[4,128,768]{2,1,0:T(8,128)(2,1)} collective-permute-done((bf16[4,128,768]{2,1,0:T(8,128)(2,1)}, bf16[4,128,768]{2,1,0:T(8,128)(2,1)}, u32[]{:S(2)}, u32[]{:S(2)}) %collective-permute-start.5) | collective-permute-done | bytes 786464 | tf_op jit(solution)/shard_map/ppermute | solution.py:27
  120.7 2.1 bitcast_dynamic-update-slice_fusion.7
  122.7 2.1 bitcast_dynamic-update-slice_fusion.6
  124.8 0.9 bitcast_dynamic-update-slice_fusion.5
  125.8 0.9 bitcast_dynamic-update-slice_fusion.4
  126.7 1.0 bitcast_dynamic-update-slice_fusion.3
  127.7 2.1 bitcast_dynamic-update-slice_fusion.2
  129.7 2.1 bitcast_dynamic-update-slice_fusion.1
  131.8 8.5 %collective-permute-done.6 = bf16[4,128,768]{2,1,0:T(8,128)(2,1)S(1)} collective-permute-done((bf16[4,128,768]{2,1,0:T(8,128)(2,1)}, bf16[4,128,768]{2,1,0:T(8,128)(2,1)S(1)}, u32[]{:S(2)}, u32[]{:S(2)}) %collective-permute-start.6) | collective-permute-done | bytes 786464 | tf_op jit(solution)/shard_map/ppermute | solution.py:27
  140.3 0.9 bitcast_dynamic-update-slice_fusion
  141.3 6.4 %gather_fusion = bf16[8,4,128,768]{3,2,1,0:T(8,128)(2,1)} fusion(bf16[8,4,128,768]{3,2,1,0:T(8,128)(2,1)} %bitcast_dynamic-update-slice_fusion, s32[1024]{0:T(1024)S(1)} %pad_clamp_fusion), kind=kCustom, calls=%fused_computation | custom fusion | bytes 12582944 | tf_op jit(solution)/shard_map/gather | solution.py:30
  147.7 9.0 %convert_bitcast_fusion = f32[4,128,8,768]{3,1,0,2:T(8,128)} fusion(bf16[8,4,128,768]{3,2,1,0:T(8,128)(2,1)} %gather_fusion), kind=kLoop, calls=%fused_computation.2 | loop fusion | flops 3145728 | bytes 18874368 | tf_op jit(solution)/shard_map/convert_element_type | solution.py:94
  156.6 1.3 fusion
  158.0 12.6 %copy.39 = f32[4,128,8,768]{1,3,2,0:T(8,128)} copy(f32[4,128,8,768]{3,1,0,2:T(8,128)} %convert_bitcast_fusion) | data formatting | bytes 25165824 | tf_op jit(solution)/shard_map/convert_element_type | solution.py:94
  170.6 9.8 %fusion.3 = bf16[4,128,6144]{1,2,0:T(8,128)(2,1)} fusion(f32[4,128,8,768]{1,3,2,0:T(8,128)} %copy.39, f32[4,6144]{1,0:T(4,128)S(1)} %copy-done.11, f32[4,6144]{1,0:T(4,128)S(1)} %get-tuple-element.13, f32[4,128]{1,0:T(4,128)S(1)} %add_rsqrt_fusion.1), kind=kLoop, calls=%fused_computation.7 | loop fusion | flops 12582912 | bytes 19073024 | tf_op jit(solution)/shard_map/convert_element_type | solution.py:95
  180.4 8.7 %copy.40 = bf16[4,128,6144]{2,1,0:T(8,128)(2,1)} copy(bf16[4,128,6144]{1,2,0:T(8,128)(2,1)} %fusion.3) | data formatting | bytes 12582912 | tf_op jit(solution)/shard_map/convert_element_type | solution.py:95
  189.1 7.6 %convolution_convert_fusion.2 = bf16[512,384]{1,0:T(8,128)(2,1)S(1)} fusion(bf16[512,6144]{1,0:T(8,128)(2,1)} %bitcast.138, bf16[6144,384]{0,1:T(8,128)(2,1)} %bitcast.139), kind=kOutput, calls=%fused_computation.29 | convolution fusion | flops 2416115712 | bytes 11403264 | tf_op jit(solution)/shard_map/dot_general | solution.py:99
  196.7 0.2 copy.42
  196.9 0.1 reshape.286
  197.0 0.8 slice.62
  197.9 1.1 copy.45
  199.0 2.4 all_gather.16
  201.4 0.7 fusion.42
  202.1 0.1 copy.51
  202.3 0.4 fusion.32
  202.7 0.8 fusion.9
  203.6 0.7 fusion.8
  204.3 0.9 divide_convert_fusion
  205.2 1.3 copy-done.4
  206.5 0.4 fusion.29
  207.0 5.4 convolution_convert_fusion.1
  212.4 0.0 all-gather.6.cloned.1.call-start
  212.5 0.5 all-gather.6.cloned.1.call-update
  213.1 0.8 dynamic-slice_bitcast_fusion.2
  213.9 116.4 %reduce-scatter.3.cloned.1.call-done = bf16[4,128,768]{2,1,0:T(8,128)(2,1)} async-done(((bf16[4,128,6144]{2,1,0:T(8,128)(2,1)}), bf16[4,128,768]{2,1,0:T(8,128)(2,1)}) %reduce-scatter.3.cloned.1.call-update) | async-done | bytes 786448 | tf_op jit(solution)/shard_map/reduce_scatter | solution.py:127
  330.2 1.5 multiply_reduce_fusion
  331.7 19.6 %psum.7 = f32[4,128]{1,0:T(4,128)S(1)} all-reduce(f32[4,128]{1,0:T(4,128)S(1)} %multiply_reduce_fusion), channel_id=1, replica_groups=mesh['rep'=2,'span'=2,'tp'=8] {'tp'}, use_global_device_ids=true, to_apply=%region_8.9 | all-reduce | flops 512 | bytes 4096 | tf_op jit(solution)/shard_map/psum | solution.py:131
  351.3 2.4 add_convert_fusion.1
  353.8 0.5 all-gather.8.cloned.1.call-update
  354.4 95.3 %all-gather.4.cloned.1.call-done = bf16[4,128,6144]{2,1,0:T(8,128)(2,1)} async-done(((bf16[4,128,768]{2,1,0:T(8,128)(2,1)}), bf16[4,128,6144]{2,1,0:T(8,128)(2,1)}) %all-gather.4.cloned.1.call-update) | async-done | bytes 6291472 | tf_op jit(solution)/shard_map/all_gather | solution.py:135
  449.7 8.2 %fusion.26 = bf16[4,128,512]{2,1,0:T(8,128)(2,1)S(1)} fusion(bf16[4,128,6144]{2,1,0:T(8,128)(2,1)} %all-gather.4.cloned.1.call-done, bf16[6144,512]{1,0:T(8,128)(2,1)} %all-gather.6.cloned.1.call-done), kind=kOutput, calls=%fused_computation.41 | convolution fusion | flops 3223584768 | bytes 13107200 | tf_op jit(solution)/shard_map/dot_general | solution.py:134
  457.9 8.3 %all-gather.8.cloned.1.call-done = bf16[512,6144]{1,0:T(8,128)(2,1)} async-done(((bf16[256,6144]{1,0:T(8,128)(2,1)}), bf16[512,6144]{1,0:T(8,128)(2,1)}) %all-gather.8.cloned.1.call-update) | async-done | bytes 6291472 | tf_op jit(solution)/shard_map/all_gather | solution.py:85
  466.2 8.1 %convolution_convert_fusion = bf16[4,128,6144]{2,1,0:T(8,128)(2,1)} fusion(bf16[4,128,512]{2,1,0:T(8,128)(2,1)S(1)} %fusion.26, bf16[512,6144]{1,0:T(8,128)(2,1)} %all-gather.8.cloned.1.call-done), kind=kOutput, calls=%fused_computation.8 | convolution fusion | flops 3224371200 | bytes 13107200 | tf_op jit(solution)/shard_map/dot_general | solution.py:140
  474.3 119.3 %reduce-scatter.5.cloned.1.call-done = bf16[4,128,768]{2,1,0:T(8,128)(2,1)} async-done(((bf16[4,128,6144]{2,1,0:T(8,128)(2,1)}), bf16[4,128,768]{2,1,0:T(8,128)(2,1)}) %reduce-scatter.5.cloned.1.call-update) | async-done | bytes 786448 | tf_op jit(solution)/shard_map/reduce_scatter | solution.py:141
  593.6 2.4 add_convert_fusion
  (53 shorter events, 0.4 us)
Async XLA Ops:
  7.4 199.6 %copy-start = (bf16[128,6144]{1,0:T(8,128)(2,1)S(1)}, bf16[128,6144]{1,0:T(8,128)(2,1)}, u32[]{:S(2)}) copy-start(bf16[128,6144]{1,0:T(8,128)(2,1)} %param.19) | copy-start | bytes 4718596
  7.4 322.8 %reduce-scatter.3.cloned.1.call-start = ((), (), s32[]{:S(2)}) async-start(), calls=%async_computation.2 | async-start | bytes 7077888 | tf_op jit(solution)/shard_map/reduce_scatter | solution.py:127
  7.4 36.9 %collective-permute-start = (bf16[4,128,768]{2,1,0:T(8,128)(2,1)}, bf16[4,128,768]{2,1,0:T(8,128)(2,1)S(1)}, u32[]{:S(2)}, u32[]{:S(2)}) collective-permute-start(bf16[4,128,768]{2,1,0:T(8,128)(2,1)} %param.11), channel_id=1, source_target_pairs={{0,1},{1,2},{2,3},{3,4},{4,5},{5,6},{6,7},{7,0},{8,9},{9,10},{10,1... | collective-permute-start | bytes 2359304 | tf_op jit(solution)/shard_map/ppermute | solution.py:25
  10.3 63.4 %collective-permute-start.4 = (bf16[4,128,768]{2,1,0:T(8,128)(2,1)}, bf16[4,128,768]{2,1,0:T(8,128)(2,1)}, u32[]{:S(2)}, u32[]{:S(2)}) collective-permute-start(bf16[4,128,768]{2,1,0:T(8,128)(2,1)} %param.11), channel_id=1, source_target_pairs={{1,0},{2,1},{3,2},{4,3},{5,4},{6,5},{7,6},{0,7},{9,8},{10,9},{11,1... | collective-permute-start | bytes 2359304 | tf_op jit(solution)/shard_map/ppermute | solution.py:27
  16.3 30.4 %copy-start.5 = (f32[4,6,6144]{2,0,1:T(4,128)}, f32[4,6,6144]{2,0,1:T(4,128)S(1)}, u32[]{:S(2)}) copy-start(f32[4,6,6144]{2,0,1:T(4,128)S(1)} %fusion.30) | copy-start | bytes 1769476
  44.3 22.1 %copy-start.7 = (bf16[4,128,768]{2,1,0:T(8,128)(2,1)}, bf16[4,128,768]{2,1,0:T(8,128)(2,1)S(1)}, u32[]{:S(2)}) copy-start(bf16[4,128,768]{2,1,0:T(8,128)(2,1)S(1)} %collective-permute-done) | copy-start | bytes 2359300
  44.3 22.1 %collective-permute-start.1 = (bf16[4,128,768]{2,1,0:T(8,128)(2,1)S(1)}, bf16[4,128,768]{2,1,0:T(8,128)(2,1)S(1)}, u32[]{:S(2)}, u32[]{:S(2)}) collective-permute-start(bf16[4,128,768]{2,1,0:T(8,128)(2,1)S(1)} %collective-permute-done), channel_id=1, source_target_pairs={{0,1},{1,2},{2,3},{3,4},{4,5},{5,6},{6,7},{7,0},{8,9},{9,10},{10,1... | collective-permute-start | bytes 2359304 | tf_op jit(solution)/shard_map/ppermute | solution.py:25
  66.4 7.0 %copy-start.9 = (bf16[4,128,768]{2,1,0:T(8,128)(2,1)}, bf16[4,128,768]{2,1,0:T(8,128)(2,1)S(1)}, u32[]{:S(2)}) copy-start(bf16[4,128,768]{2,1,0:T(8,128)(2,1)S(1)} %collective-permute-done.1) | copy-start | bytes 2359300
  66.4 32.4 %collective-permute-start.2 = (bf16[4,128,768]{2,1,0:T(8,128)(2,1)S(1)}, bf16[4,128,768]{2,1,0:T(8,128)(2,1)}, u32[]{:S(2)}, u32[]{:S(2)}) collective-permute-start(bf16[4,128,768]{2,1,0:T(8,128)(2,1)S(1)} %collective-permute-done.1), channel_id=1, source_target_pairs={{0,1},{1,2},{2,3},{3,4},{4,5},{5,6},{6,7},{7,0},{8,9},{9,10},{10,1... | collective-permute-start | bytes 2359304 | tf_op jit(solution)/shard_map/ppermute | solution.py:25
  66.4 7.1 %copy-start.14 = (s32[8]{0:T(128)S(1)}, s32[8]{0:T(128)}, u32[]{:S(2)}) copy-start(s32[8]{0:T(128)} %param.13) | copy-start | bytes 100
  66.4 35.1 %copy-start.12 = (bf16[4,128,2,128]{3,2,1,0:T(2,128)(2,1)S(1)}, bf16[4,128,2,128]{3,2,1,0:T(2,128)(2,1)}, u32[]{:S(2)}) copy-start(bf16[4,128,2,128]{3,2,1,0:T(2,128)(2,1)} %param.16) | copy-start | bytes 786436
  73.4 53.3 %copy-start.2 = (bf16[4,128,768]{2,1,0:T(8,128)(2,1)S(1)}, bf16[4,128,768]{2,1,0:T(8,128)(2,1)}, u32[]{:S(2)}) copy-start(bf16[4,128,768]{2,1,0:T(8,128)(2,1)} %param.11) | copy-start | bytes 2359300
  73.8 46.9 %collective-permute-start.5 = (bf16[4,128,768]{2,1,0:T(8,128)(2,1)}, bf16[4,128,768]{2,1,0:T(8,128)(2,1)}, u32[]{:S(2)}, u32[]{:S(2)}) collective-permute-start(bf16[4,128,768]{2,1,0:T(8,128)(2,1)} %collective-permute-done.4), channel_id=1, source_target_pairs={{1,0},{2,1},{3,2},{4,3},{5,4},{6,5},{7,6},{0,7},{9,8},{10,9},{11,1... | collective-permute-start | bytes 2359304 | tf_op jit(solution)/shard_map/ppermute | solution.py:27
  98.8 21.9 %collective-permute-start.3 = (bf16[4,128,768]{2,1,0:T(8,128)(2,1)}, bf16[4,128,768]{2,1,0:T(8,128)(2,1)}, u32[]{:S(2)}, u32[]{:S(2)}) collective-permute-start(bf16[4,128,768]{2,1,0:T(8,128)(2,1)} %collective-permute-done.2), channel_id=1, source_target_pairs={{0,1},{1,2},{2,3},{3,4},{4,5},{5,6},{6,7},{7,0},{8,9},{9,10},{10,1... | collective-permute-start | bytes 2359304 | tf_op jit(solution)/shard_map/ppermute | solution.py:25
  101.5 23.3 %copy-start.10 = (bf16[4,128,768]{2,1,0:T(8,128)(2,1)S(1)}, bf16[4,128,768]{2,1,0:T(8,128)(2,1)}, u32[]{:S(2)}) copy-start(bf16[4,128,768]{2,1,0:T(8,128)(2,1)} %copy-done.9) | copy-start | bytes 2359300
  101.6 24.2 %copy-start.8 = (bf16[4,128,768]{2,1,0:T(8,128)(2,1)S(1)}, bf16[4,128,768]{2,1,0:T(8,128)(2,1)}, u32[]{:S(2)}) copy-start(bf16[4,128,768]{2,1,0:T(8,128)(2,1)} %copy-done.7) | copy-start | bytes 2359300
  120.7 19.7 %collective-permute-start.6 = (bf16[4,128,768]{2,1,0:T(8,128)(2,1)}, bf16[4,128,768]{2,1,0:T(8,128)(2,1)S(1)}, u32[]{:S(2)}, u32[]{:S(2)}) collective-permute-start(bf16[4,128,768]{2,1,0:T(8,128)(2,1)} %collective-permute-done.5), channel_id=1, source_target_pairs={{1,0},{2,1},{3,2},{4,3},{5,4},{6,5},{7,6},{0,7},{9,8},{10,9},{11,1... | collective-permute-start | bytes 2359304 | tf_op jit(solution)/shard_map/ppermute | solution.py:27
  147.7 9.0 %copy-start.1 = (bf16[8,4,128,768]{3,2,1,0:T(8,128)(2,1)S(1)}, bf16[8,4,128,768]{3,2,1,0:T(8,128)(2,1)}, u32[]{:S(2)}) copy-start(bf16[8,4,128,768]{3,2,1,0:T(8,128)(2,1)} %gather_fusion) | copy-start | bytes 18874372
  157.9 12.6 %copy-start.11 = (f32[4,6144]{1,0:T(4,128)S(1)}, f32[4,6144]{1,0:T(4,128)}, u32[]{:S(2)}) copy-start(f32[4,6144]{1,0:T(4,128)} %get-tuple-element.14) | copy-start | bytes 294916
  197.0 5.7 copy-start.6
  203.5 3.0 copy-start.13
  205.2 1.3 copy-start.4
  212.4 142.0 %all-gather.6.cloned.1.call-start = ((), (), s32[]{:S(2)}) async-start(), calls=%async_computation.4 | async-start | bytes 9437184 | tf_op jit(solution)/shard_map/all_gather | solution.py:84
  213.0 236.7 %all-gather.4.cloned.1.call-start = ((), (), s32[]{:S(2)}) async-start(), calls=%async_computation.3 | async-start | bytes 7077888 | tf_op jit(solution)/shard_map/all_gather | solution.py:135
  353.8 112.4 %all-gather.8.cloned.1.call-start = ((), (), s32[]{:S(2)}) async-start(), calls=%async_computation.5 | async-start | bytes 9437184 | tf_op jit(solution)/shard_map/all_gather | solution.py:85
  354.4 239.2 %reduce-scatter.5.cloned.1.call-start = ((), (), s32[]{:S(2)}) async-start(), calls=%async_computation.6 | async-start | bytes 7077888 | tf_op jit(solution)/shard_map/reduce_scatter | solution.py:141
  474.3 119.3 %copy-start.3 = (bf16[4,128,768]{2,1,0:T(8,128)(2,1)S(1)}, bf16[4,128,768]{2,1,0:T(8,128)(2,1)}, u32[]{:S(2)}) copy-start(bf16[4,128,768]{2,1,0:T(8,128)(2,1)} %reduce-scatter.3.cloned.1.call-done) | copy-start | bytes 2359300
Sparse Core Ops, SparseCore 0:
  212.6 117.5 reduce-scatter.2
  474.4 119.1 reduce-scatter.4
Sparse Core Ops, SparseCore 1:
  214.5 15.2 all-gather.5
  353.9 95.8 all-gather.3
  451.1 15.0 all-gather.7
